TPU v7x, 512 devices: a whole 4x8x8 slice. The times are simulated.
512 devices in a mesh: band: 32 (over x, y), seq: 16 (over z, core).
Axes of the slice: x: 4, y: 8, z: 8, core: 2. Of those that a mesh axis runs over, the one named last changes fastest.
Arguments:
- posteriors: bfloat16 [32, 262144], P(None, ('band', 'seq'))
- seed_mask: int32 [262144], P(('band', 'seq')), may hold values 0 or 1
- frame_perm: int32 [512, 512], P(('band', 'seq')), may hold values from 0 to 511, each once within a row
- lengths: int32 [256], replicated, may hold values from 1 to 4096, 262144 in all
- embeddings: bfloat16 [262144, 256], P(('band', 'seq')), may hold values from -12 to 12
- partners: int32 [2048, 32], P(('band', 'seq')), may hold values from 0 to 127, as said below
- levels: int32 [2048, 32], P(('band', 'seq')), may hold values from 1 to 8, as said below
Outputs:
- spread_labels: float32 [32, 262144], P(None, ('band', 'seq'))
Inputs may be any that keep to these rules, and one draw needn't show every extreme that they name: `partners`: within each seq index s, slot k pairs the 128 tiles mutually: if tile number a names b in slot k then b names a in slot k; no tile names itself. `levels`: two tiles paired in slot k carry the same level.
All inputs are finite; a program needn't handle non-finite values. No bound on the sum of `seed_mask` on one device may be relied on, other than what follows from the above.
Results may differ from a plain program's by a relative error of at most 0.007.
Values may be sent and summed in bfloat16 or wider, within the bound.
No kernel may reach another device: no remote copies, remote signals or barrier semaphores. Data moves between devices by JAX's collectives and lax.ppermute only.
A program may use at most 64 MiB of HBM per device.

v0:
```python
import math
import jax
import jax.numpy as jnp
from jax import lax
from jax.sharding import PartitionSpec as P

RADIUS = 64
ITERS = 3
decay_len = 16.0
spread_rate = 0.9


def with_halo(cells, sides, width):
    for axis, dim in sides:
        count = lax.axis_size(axis)
        ends = count - 1
        head = lax.slice_in_dim(cells, 0, width, axis=dim)
        tail = lax.slice_in_dim(cells, cells.shape[dim] - width, cells.shape[dim], axis=dim)
        cells = jnp.concatenate(
            [
                lax.ppermute(tail, axis, [(i, (i + 1) % count) for i in range(ends)]),
                cells,
                lax.ppermute(head, axis, [((i + 1) % count, i) for i in range(ends)]),
            ],
            axis=dim,
        )
    return cells


def total_over_devices(values):
    for axis in ("seq", "band"):
        count = lax.axis_size(axis)
        spread = jnp.broadcast_to(values[None], (count,) + values.shape)
        rows = lax.all_to_all(spread, axis, split_axis=0, concat_axis=0, tiled=True)
        values = jnp.sum(rows, axis=0)
    return values


def band_gather(block):
    count = lax.axis_size("band")
    spread = jnp.broadcast_to(block[None], (count,) + block.shape)
    return lax.all_to_all(spread, "band", split_axis=0, concat_axis=0, tiled=True)


def on_device(posteriors, seed_mask, frame_perm, lengths, embeddings, partners, levels):
    channels, frames = posteriors.shape
    band_count = lax.axis_size("band")
    groups = lax.axis_size("seq")
    tile_count = frames // 128
    seeded = posteriors * seed_mask.astype(jnp.bfloat16)[None, :]
    ordered = jnp.take(seeded, frame_perm[0], axis=1).reshape(
        channels, band_count, frames // band_count
    )
    arrived = lax.all_to_all(ordered, "band", split_axis=1, concat_axis=1, tiled=True)
    labels = arrived.reshape(channels, frames).astype(jnp.float32)
    device = lax.axis_index("band") * groups + lax.axis_index("seq")
    frame_total = frames * band_count * groups
    window = 128 + 2 * RADIUS
    global_at = device * frames - RADIUS + jnp.arange(frames + 2 * RADIUS, dtype=jnp.int32)
    utt_ends = jnp.cumsum(lengths)
    owner_seg = jnp.sum((utt_ends[None, :] <= global_at[:, None]).astype(jnp.int32), axis=1)
    inside = (global_at >= 0) & (global_at < frame_total)
    tile_off = (jnp.arange(tile_count, dtype=jnp.int32) * 128)[:, None, None]
    win_pos = tile_off + jnp.arange(window, dtype=jnp.int32)[None, :, None]
    row_pos = tile_off + RADIUS + jnp.arange(128, dtype=jnp.int32)[None, None, :]
    offset = jnp.abs(win_pos - row_pos)
    linked = (
        (offset >= 1)
        & (offset <= RADIUS)
        & (owner_seg[win_pos] == owner_seg[row_pos])
        & inside[win_pos]
    )
    band_tiles = jnp.where(
        linked, jnp.exp(-offset.astype(jnp.float32) / decay_len), jnp.float32(0.0)
    ).astype(jnp.bfloat16)
    near_degree = jnp.sum(band_tiles.astype(jnp.float32), axis=1).reshape(frames)
    gathered = lax.all_gather(embeddings, "band", axis=0, tiled=True)
    labels_band = band_gather(arrived.reshape(channels, frames))
    labels_band, gathered = lax.optimization_barrier((labels_band, gathered))
    embed_width = embeddings.shape[1]
    partner_rows = gathered.reshape(-1, 128, embed_width)[partners]
    own_rows = embeddings.reshape(tile_count, 128, embed_width)
    inner_prod = jnp.einsum(
        "tkje,tie->tkji", partner_rows, own_rows, preferred_element_type=jnp.float32
    )
    affinity = (
        jnp.exp(0.5 * (inner_prod / math.sqrt(embed_width)))
        * (levels.astype(jnp.float32) / 8.0)[:, :, None, None]
        / 128.0
    )
    affinity = affinity.astype(jnp.bfloat16)
    far_degree = jnp.sum(affinity.astype(jnp.float32), axis=(1, 2)).reshape(frames)
    norm_scale = 1.0 / jnp.sqrt(near_degree + far_degree)

    def squares(residual):
        return total_over_devices(jnp.sum(residual * residual, axis=1))

    solution = jnp.zeros((channels, frames), jnp.float32)
    residual = labels
    direction = labels
    first_norm = jnp.sum(residual * residual, axis=1)
    scale_band = band_gather(norm_scale)
    for iteration in range(ITERS):
        lifted = (norm_scale[None, :] * direction).astype(jnp.bfloat16)
        padded = with_halo(lifted, ((("band", "seq"), 1),), RADIUS)
        windows = jnp.stack(
            [padded[:, position * 128 : position * 128 + window] for position in range(tile_count)],
            axis=0,
        )
        near_term = jnp.einsum(
            "tcw,twa->cta", windows, band_tiles, preferred_element_type=jnp.float32
        ).reshape(channels, frames)
        if iteration == 0:
            lifted_band = (scale_band[:, None, :] * labels_band.astype(jnp.float32)).astype(
                jnp.bfloat16
            )
        else:
            lifted_band = band_gather(lifted)
        spread = jnp.transpose(lifted_band, (1, 0, 2)).reshape(channels, -1, 128)
        far_tiles = spread[:, partners]
        far_term = jnp.einsum(
            "ctkj,tkji->cti", far_tiles, affinity, preferred_element_type=jnp.float32
        ).reshape(channels, frames)
        image = direction - spread_rate * norm_scale[None, :] * (near_term + far_term)
        sums = [jnp.sum(direction * image, axis=1)]
        last = iteration == ITERS - 1
        if not last:
            sums += [jnp.sum(residual * image, axis=1), jnp.sum(image * image, axis=1)]
        if iteration == 0:
            sums.append(first_norm)
        totals = total_over_devices(jnp.stack(sums))
        curve = totals[0]
        if iteration == 0:
            norm_now = totals[-1]
        alpha = norm_now / curve
        solution = solution + alpha[:, None] * direction
        if not last:
            residual = residual - alpha[:, None] * image
            norm_next = norm_now - 2.0 * alpha * totals[1] + alpha * alpha * totals[2]
            direction = residual + (norm_next / norm_now)[:, None] * direction
            norm_now = norm_next
    return solution


def solution(mesh):
    placed = (
        P(None, ("band", "seq")),
        P(("band", "seq")),
        P(("band", "seq"), None),
        P(),
        P(("band", "seq"), None),
        P(("band", "seq"), None),
        P(("band", "seq"), None),
    )
    return jax.shard_map(
        on_device, mesh=mesh, in_specs=placed, out_specs=P(None, ("band", "seq")), check_vma=False
    )
```

profile of v0, /device:TPU:1, one launch (start us, length us, event | category | flops | bytes accessed | tf_op | source)
XLA Modules:
  0.0 341.7 jit_solution(14593774616092935248)
XLA Ops:
  6.5 0.7 all-gather.2.cloned.1.call-update
  7.3 0.7 convert_element_type.66
  7.9 0.8 broadcast_multiply_fusion
  9.4 1.3 reduce.14
  10.8 0.7 compare_select_fusion.1
  11.5 1.3 gather_fusion
  13.0 0.8 reshape.829
  13.7 10.5 %all-to-all-start = ((bf16[32,2,256]{2,1,0:T(2,128)(2,1)}), bf16[32,2,256]{2,1,0:T(2,128)(2,1)S(1)}, u32[]{:S(2)}, u32[]{:S(2)}) async-start(bf16[32,2,256]{2,1,0:T(2,128)(2,1)} %reshape.829), calls=%async_computation | async-start | bytes 65536 | tf_op jit(solution)/shard_map/all_to_all | solution.py:54
  24.3 1.0 reduce-window.9
  25.6 7.4 %all-to-all-done = bf16[32,2,256]{2,1,0:T(2,128)(2,1)S(1)} async-done(((bf16[32,2,256]{2,1,0:T(2,128)(2,1)}), bf16[32,2,256]{2,1,0:T(2,128)(2,1)S(1)}, u32[]{:S(2)}, u32[]{:S(2)}) %all-to-all-start) | async-done | bytes 32800 | tf_op jit(solution)/shard_map/all_to_all | solution.py:54
  33.2 1.2 broadcast_in_dim.40
  34.4 3.9 %all-to-all-start.1 = ((bf16[32,32,512]{2,1,0:T(8,128)(2,1)}), bf16[32,32,512]{2,1,0:T(8,128)(2,1)S(1)}, u32[]{:S(2)}, u32[]{:S(2)}) async-start(bf16[32,32,512]{2,1,0:T(8,128)(2,1)} %broadcast_in_dim.40), calls=%async_computation.1 | async-start | bytes 2097152 | tf_op jit(solution)/shard_map/all_to_all | solution.py:42
  38.7 4.5 %gather_fusion.1 = s32[1024]{0:T(1024)S(1)} fusion(s32[640]{0:T(1024)S(1)} %convert_reduce_fusion.1, s32[1024]{0:T(1024)S(1)} %broadcast_clamp_fusion), kind=kCustom, calls=%fused_computation.1 | custom fusion | bytes 12288 | tf_op jit(solution)/shard_map/gather | solution.py:70
  43.3 2.3 gather_fusion.2
  45.6 6.8 %gather_fusion.3 = pred[1024]{0:T(1024)(128)(4,1)S(1)} fusion(pred[640]{0:T(1024)(128)(4,1)S(1)} %compare_and_fusion.1, s32[1024]{0:T(1024)S(1)} %broadcast_clamp_fusion), kind=kCustom, calls=%fused_computation.3 | custom fusion | bytes 6144 | tf_op jit(solution)/shard_map/gather | solution.py:71
  53.3 16.7 %all-to-all-done.1 = bf16[32,32,512]{2,1,0:T(8,128)(2,1)S(1)} async-done(((bf16[32,32,512]{2,1,0:T(8,128)(2,1)}), bf16[32,32,512]{2,1,0:T(8,128)(2,1)S(1)}, u32[]{:S(2)}, u32[]{:S(2)}) %all-to-all-start.1) | async-done | bytes 1048608 | tf_op jit(solution)/shard_map/all_to_all | solution.py:42
  70.0 58.1 %all-gather.2.cloned.1.call-done = bf16[16384,256]{1,0:T(8,128)(2,1)} async-done(((bf16[512,256]{1,0:T(8,128)(2,1)}), bf16[16384,256]{1,0:T(8,128)(2,1)}) %all-gather.2.cloned.1.call-update) | async-done | bytes 8388624 | tf_op jit(solution)/shard_map/all_gather | solution.py:77
  128.2 10.0 %gather_fusion.4 = bf16[128,128,256]{2,1,0:T(8,128)(2,1)} fusion(bf16[128,128,256]{2,1,0:T(8,128)(2,1)} %bitcast.181, s32[1024]{0:T(1024)S(1)} %pad_clamp_fusion), kind=kCustom, calls=%fused_computation.4 | custom fusion | bytes 16777728 | tf_op jit(solution)/shard_map/gather | solution.py:81
  138.1 7.7 %convert_reduce_fusion = (f32[4,128]{1,0:T(4,128)S(1)}, bf16[4,32,128,128]{3,2,1,0:T(8,128)(2,1)}) fusion(f32[4,32]{1,0:T(4,128)S(1)} %convert_multiply_fusion.6, bf16[4,32,128,256]{3,2,1,0:T(8,128)(2,1)} %bitcast.182, bf16[4,128,256,1]{2,1,3,0:T(8,128)(2,1)S(1)} %bitcast.198), kind=kOutput, calls=%fused_computation.8 | convolution fusion | flops 1086324224 | bytes 12847616 | tf_op jit(solution)/shard_map/tkje,tie->tkji/dot_general | solution.py:83
  145.9 4.2 %collective-permute-start = (bf16[32,64]{1,0:T(8,128)(2,1)S(1)}, bf16[32,64]{1,0:T(8,128)(2,1)S(1)}, u32[]{:S(2)}, u32[]{:S(2)}) collective-permute-start(bf16[32,64]{1,0:T(8,128)(2,1)S(1)} %get-tuple-element.41), channel_id=1, source_target_pairs={{0,1},{1,2},{2,3},{3,4},{4,5},{5,6},{6,7},{7,8},{8,9},{9,10},{10,1... | collective-permute-start | bytes 12296 | tf_op jit(solution)/shard_map/ppermute | solution.py:21
  150.2 1.9 collective-permute-start.1
  152.8 5.7 %all-to-all-start.2 = ((f32[32,1,512]{2,1,0:T(1,128)}), f32[32,1,512]{2,1,0:T(1,128)S(1)}, u32[]{:S(2)}, u32[]{:S(2)}) async-start(f32[32,1,512]{2,1,0:T(1,128)} %mul.397), calls=%async_computation.2 | async-start | bytes 131072 | tf_op jit(solution)/shard_map/all_to_all | solution.py:42
  159.2 7.9 %all-to-all-done.2 = f32[32,1,512]{2,1,0:T(1,128)S(1)} async-done(((f32[32,1,512]{2,1,0:T(1,128)}), f32[32,1,512]{2,1,0:T(1,128)S(1)}, u32[]{:S(2)}, u32[]{:S(2)}) %all-to-all-start.2) | async-done | bytes 65568 | tf_op jit(solution)/shard_map/all_to_all | solution.py:42
  169.3 0.8 gather_fusion.5
  170.1 2.9 fusion.3
  173.5 17.3 %all_to_all.56 = f32[16,1,128]{2,1,0:T(1,128)S(1)} all-to-all(f32[16,1,128]{2,1,0:T(1,128)S(1)} %reshape.831), channel_id=1, replica_groups=mesh['band'=32,'seq'=16] {'seq'}, dimensions={0} | all-to-all | bytes 16384 | tf_op jit(solution)/shard_map/all_to_all | solution.py:34
  192.2 11.6 %all_to_all.57 = f32[32,1,128]{2,1,0:T(1,128)S(1)} all-to-all(f32[32,1,128]{2,1,0:T(1,128)S(1)} %reshape.833), channel_id=1, replica_groups=mesh['band'=32,'seq'=16] {'band'}, dimensions={0} | all-to-all | bytes 32768 | tf_op jit(solution)/shard_map/all_to_all | solution.py:34
  204.8 1.1 broadcast_in_dim.44
  205.9 3.9 %all-to-all-start.5 = ((bf16[32,32,512]{2,1,0:T(8,128)(2,1)}), bf16[32,32,512]{2,1,0:T(8,128)(2,1)S(1)}, u32[]{:S(2)}, u32[]{:S(2)}) async-start(bf16[32,32,512]{2,1,0:T(8,128)(2,1)} %broadcast_in_dim.44), calls=%async_computation.5 | async-start | bytes 2097152 | tf_op jit(solution)/shard_map/all_to_all | solution.py:42
  209.9 4.0 %collective-permute-start.2 = (bf16[32,64]{1,0:T(8,128)(2,1)S(1)}, bf16[32,64]{1,0:T(8,128)(2,1)S(1)}, u32[]{:S(2)}, u32[]{:S(2)}) collective-permute-start(bf16[32,64]{1,0:T(8,128)(2,1)S(1)} %get-tuple-element.35), channel_id=1, source_target_pairs={{0,1},{1,2},{2,3},{3,4},{4,5},{5,6},{6,7},{7,8},{8,9},{9,10},{10,1... | collective-permute-start | bytes 12296 | tf_op jit(solution)/shard_map/ppermute | solution.py:21
  213.9 1.9 collective-permute-start.3
  215.8 3.3 collective-permute-done.3
  219.9 14.5 %all-to-all-done.5 = bf16[32,32,512]{2,1,0:T(8,128)(2,1)S(1)} async-done(((bf16[32,32,512]{2,1,0:T(8,128)(2,1)}), bf16[32,32,512]{2,1,0:T(8,128)(2,1)S(1)}, u32[]{:S(2)}, u32[]{:S(2)}) %all-to-all-start.5) | async-done | bytes 1048608 | tf_op jit(solution)/shard_map/all_to_all | solution.py:42
  236.3 0.8 gather_fusion.6
  237.0 2.9 fusion.2
  240.4 15.1 %all_to_all.58 = f32[16,3,32]{2,1,0:T(4,128)S(1)} all-to-all(f32[16,3,32]{2,1,0:T(4,128)S(1)} %broadcast_in_dim.45), channel_id=1, replica_groups=mesh['band'=32,'seq'=16] {'seq'}, dimensions={0} | all-to-all | bytes 12288 | tf_op jit(solution)/shard_map/all_to_all | solution.py:34
  255.5 14.1 %all_to_all.59 = f32[32,3,32]{2,1,0:T(4,128)S(1)} all-to-all(f32[32,3,32]{2,1,0:T(4,128)S(1)} %broadcast_in_dim.46), channel_id=1, replica_groups=mesh['band'=32,'seq'=16] {'band'}, dimensions={0} | all-to-all | bytes 24576 | tf_op jit(solution)/shard_map/all_to_all | solution.py:34
  269.8 1.1 broadcast_in_dim.47
  270.9 3.9 %all-to-all-start.8 = ((bf16[32,32,512]{2,1,0:T(8,128)(2,1)}), bf16[32,32,512]{2,1,0:T(8,128)(2,1)S(1)}, u32[]{:S(2)}, u32[]{:S(2)}) async-start(bf16[32,32,512]{2,1,0:T(8,128)(2,1)} %broadcast_in_dim.47), calls=%async_computation.8 | async-start | bytes 2097152 | tf_op jit(solution)/shard_map/all_to_all | solution.py:42
  274.9 3.9 %collective-permute-start.4 = (bf16[32,64]{1,0:T(8,128)(2,1)S(1)}, bf16[32,64]{1,0:T(8,128)(2,1)S(1)}, u32[]{:S(2)}, u32[]{:S(2)}) collective-permute-start(bf16[32,64]{1,0:T(8,128)(2,1)S(1)} %get-tuple-element.29), channel_id=1, source_target_pairs={{0,1},{1,2},{2,3},{3,4},{4,5},{5,6},{6,7},{7,8},{8,9},{9,10},{10,1... | collective-permute-start | bytes 12296 | tf_op jit(solution)/shard_map/ppermute | solution.py:21
  278.8 2.1 collective-permute-start.5
  280.9 3.1 collective-permute-done.5
  284.7 14.7 %all-to-all-done.8 = bf16[32,32,512]{2,1,0:T(8,128)(2,1)S(1)} async-done(((bf16[32,32,512]{2,1,0:T(8,128)(2,1)}), bf16[32,32,512]{2,1,0:T(8,128)(2,1)S(1)}, u32[]{:S(2)}, u32[]{:S(2)}) %all-to-all-start.8) | async-done | bytes 1048608 | tf_op jit(solution)/shard_map/all_to_all | solution.py:42
  301.4 0.8 gather_fusion.7
  302.1 2.9 fusion.1
  305.5 14.7 %all_to_all.60 = f32[16,1,32]{2,1,0:T(1,128)S(1)} all-to-all(f32[16,1,32]{2,1,0:T(1,128)S(1)} %broadcast_in_dim.48), channel_id=1, replica_groups=mesh['band'=32,'seq'=16] {'seq'}, dimensions={0} | all-to-all | bytes 4096 | tf_op jit(solution)/shard_map/all_to_all | solution.py:34
  320.2 13.9 %all_to_all.61 = f32[32,1,32]{2,1,0:T(1,128)S(1)} all-to-all(f32[32,1,32]{2,1,0:T(1,128)S(1)} %broadcast_in_dim.49), channel_id=1, replica_groups=mesh['band'=32,'seq'=16] {'band'}, dimensions={0} | all-to-all | bytes 8192 | tf_op jit(solution)/shard_map/all_to_all | solution.py:34
  334.1 0.7 fusion.19
  (99 shorter events, 15.5 us)
Async XLA Ops:
  6.5 45.9 %copy-start.1 = (s32[4,32]{1,0:T(4,128)S(1)}, s32[4,32]{1,0:T(4,128)}, u32[]{:S(2)}) copy-start(s32[4,32]{1,0:T(4,128)} %param.12) | copy-start | bytes 1540
  6.5 46.7 %copy-start.2 = (s32[4,32]{1,0:T(4,128)S(1)}, s32[4,32]{1,0:T(4,128)}, u32[]{:S(2)}) copy-start(s32[4,32]{1,0:T(4,128)} %param.13) | copy-start | bytes 1540
  6.5 121.6 %all-gather.2.cloned.1.call-start = ((), (), s32[]{:S(2)}) async-start(), calls=%async_computation.11 | async-start | bytes 8650752 | tf_op jit(solution)/shard_map/all_gather | solution.py:77
  13.7 19.3 %all-to-all-start = ((bf16[32,2,256]{2,1,0:T(2,128)(2,1)}), bf16[32,2,256]{2,1,0:T(2,128)(2,1)S(1)}, u32[]{:S(2)}, u32[]{:S(2)}) async-start(bf16[32,2,256]{2,1,0:T(2,128)(2,1)} %reshape.829), calls=%async_computation | async-start | bytes 65536 | tf_op jit(solution)/shard_map/all_to_all | solution.py:54
  34.4 35.6 %all-to-all-start.1 = ((bf16[32,32,512]{2,1,0:T(8,128)(2,1)}), bf16[32,32,512]{2,1,0:T(8,128)(2,1)S(1)}, u32[]{:S(2)}, u32[]{:S(2)}) async-start(bf16[32,32,512]{2,1,0:T(8,128)(2,1)} %broadcast_in_dim.40), calls=%async_computation.1 | async-start | bytes 2097152 | tf_op jit(solution)/shard_map/all_to_all | solution.py:42
  128.1 10.0 %copy-start = (bf16[512,256]{1,0:T(8,128)(2,1)S(1)}, bf16[512,256]{1,0:T(8,128)(2,1)}, u32[]{:S(2)}) copy-start(bf16[512,256]{1,0:T(8,128)(2,1)} %param.11) | copy-start | bytes 786436
  145.9 12.6 %collective-permute-start = (bf16[32,64]{1,0:T(8,128)(2,1)S(1)}, bf16[32,64]{1,0:T(8,128)(2,1)S(1)}, u32[]{:S(2)}, u32[]{:S(2)}) collective-permute-start(bf16[32,64]{1,0:T(8,128)(2,1)S(1)} %get-tuple-element.41), channel_id=1, source_target_pairs={{0,1},{1,2},{2,3},{3,4},{4,5},{5,6},{6,7},{7,8},{8,9},{9,10},{10,1... | collective-permute-start | bytes 12296 | tf_op jit(solution)/shard_map/ppermute | solution.py:21
  150.2 8.4 %collective-permute-start.1 = (bf16[32,64]{1,0:T(8,128)(2,1)S(1)}, bf16[32,64]{1,0:T(8,128)(2,1)S(1)}, u32[]{:S(2)}, u32[]{:S(2)}) collective-permute-start(bf16[32,64]{1,0:T(8,128)(2,1)S(1)} %get-tuple-element.42), channel_id=1, source_target_pairs={{1,0},{2,1},{3,2},{4,3},{5,4},{6,5},{7,6},{8,7},{9,8},{10,9},{11,1... | collective-permute-start | bytes 12296 | tf_op jit(solution)/shard_map/ppermute | solution.py:23
  152.8 14.4 %all-to-all-start.2 = ((f32[32,1,512]{2,1,0:T(1,128)}), f32[32,1,512]{2,1,0:T(1,128)S(1)}, u32[]{:S(2)}, u32[]{:S(2)}) async-start(f32[32,1,512]{2,1,0:T(1,128)} %mul.397), calls=%async_computation.2 | async-start | bytes 131072 | tf_op jit(solution)/shard_map/all_to_all | solution.py:42
  205.9 28.5 %all-to-all-start.5 = ((bf16[32,32,512]{2,1,0:T(8,128)(2,1)}), bf16[32,32,512]{2,1,0:T(8,128)(2,1)S(1)}, u32[]{:S(2)}, u32[]{:S(2)}) async-start(bf16[32,32,512]{2,1,0:T(8,128)(2,1)} %broadcast_in_dim.44), calls=%async_computation.5 | async-start | bytes 2097152 | tf_op jit(solution)/shard_map/all_to_all | solution.py:42
  209.9 6.0 %collective-permute-start.2 = (bf16[32,64]{1,0:T(8,128)(2,1)S(1)}, bf16[32,64]{1,0:T(8,128)(2,1)S(1)}, u32[]{:S(2)}, u32[]{:S(2)}) collective-permute-start(bf16[32,64]{1,0:T(8,128)(2,1)S(1)} %get-tuple-element.35), channel_id=1, source_target_pairs={{0,1},{1,2},{2,3},{3,4},{4,5},{5,6},{6,7},{7,8},{8,9},{9,10},{10,1... | collective-permute-start | bytes 12296 | tf_op jit(solution)/shard_map/ppermute | solution.py:21
  213.9 5.3 %collective-permute-start.3 = (bf16[32,64]{1,0:T(8,128)(2,1)S(1)}, bf16[32,64]{1,0:T(8,128)(2,1)S(1)}, u32[]{:S(2)}, u32[]{:S(2)}) collective-permute-start(bf16[32,64]{1,0:T(8,128)(2,1)S(1)} %get-tuple-element.36), channel_id=1, source_target_pairs={{1,0},{2,1},{3,2},{4,3},{5,4},{6,5},{7,6},{8,7},{9,8},{10,9},{11,1... | collective-permute-start | bytes 12296 | tf_op jit(solution)/shard_map/ppermute | solution.py:23
  270.9 28.5 %all-to-all-start.8 = ((bf16[32,32,512]{2,1,0:T(8,128)(2,1)}), bf16[32,32,512]{2,1,0:T(8,128)(2,1)S(1)}, u32[]{:S(2)}, u32[]{:S(2)}) async-start(bf16[32,32,512]{2,1,0:T(8,128)(2,1)} %broadcast_in_dim.47), calls=%async_computation.8 | async-start | bytes 2097152 | tf_op jit(solution)/shard_map/all_to_all | solution.py:42
  274.9 6.0 %collective-permute-start.4 = (bf16[32,64]{1,0:T(8,128)(2,1)S(1)}, bf16[32,64]{1,0:T(8,128)(2,1)S(1)}, u32[]{:S(2)}, u32[]{:S(2)}) collective-permute-start(bf16[32,64]{1,0:T(8,128)(2,1)S(1)} %get-tuple-element.29), channel_id=1, source_target_pairs={{0,1},{1,2},{2,3},{3,4},{4,5},{5,6},{6,7},{7,8},{8,9},{9,10},{10,1... | collective-permute-start | bytes 12296 | tf_op jit(solution)/shard_map/ppermute | solution.py:21
  278.8 5.3 %collective-permute-start.5 = (bf16[32,64]{1,0:T(8,128)(2,1)S(1)}, bf16[32,64]{1,0:T(8,128)(2,1)S(1)}, u32[]{:S(2)}, u32[]{:S(2)}) collective-permute-start(bf16[32,64]{1,0:T(8,128)(2,1)S(1)} %get-tuple-element.30), channel_id=1, source_target_pairs={{1,0},{2,1},{3,2},{4,3},{5,4},{6,5},{7,6},{8,7},{9,8},{10,9},{11,1... | collective-permute-start | bytes 12296 | tf_op jit(solution)/shard_map/ppermute | solution.py:23
Sparse Core Ops, SparseCore 0:
  10.5 117.5 all-gather.1
where the time goes:
time: 343 us; the launch traced here: 342 us
  waiting for transfers between devices  126 us (37%)
  blocking collectives  86.7 us (25%)
  starting transfers between devices  46.1 us (13%)
  local copies, waits for them, and re-layouts  40.7 us (12%)
  matrix products  18.3 us (5%)
  between operations  13.9 us (4%)
  other arithmetic  9.58 us (3%)
    all_to_all x6, blocking collectives, total_over_devices(): rows = lax.all_to_all(spread, axis, split_axis=0, concat_axis=0, tiled=True)  86.7 us
    all_gather x1, waiting for transfers between devices, on_device(): gathered = lax.all_gather(embeddings, 'band', axis=0, tiled=True)  58.1 us
    all_to_all x4, waiting for transfers between devices, band_gather(): lax.all_to_all(spread, 'band', split_axis=0, concat_axis=0, tiled=True)  53.8 us
    all_to_all x4, starting transfers between devices, band_gather(): lax.all_to_all(spread, 'band', split_axis=0, concat_axis=0, tiled=True)  17.5 us
    ppermute x3, starting transfers between devices, with_halo(): lax.ppermute(tail, axis, [(i, (i + 1) % count) for i in range(ends)])  12.1 us
    all_to_all x1, starting transfers between devices, on_device(): lax.all_to_all(ordered, 'band', split_axis=1, concat_axis=1, tiled=True)  10.5 us
    gather x1, local copies, waits for them, and re-layouts, on_device(): partner_rows = gathered.reshape(-1, 128, embed_width)[partners]  9.99 us
    dot_general x3, matrix products, on_device(): jnp.einsum('ctkj,tkji->cti', far_tiles, affinity, preferred_element_type=...  8.82 us
  transfers between devices with their start and end apart: 12, of which 8 were waited for; matrix products, arithmetic and copies ran while one was open for 8% of the time, Pallas kernels for 0%

commit v1 on v0

--- a/solution.py
+++ b/solution.py
@@ -74,7 +74,11 @@
         linked, jnp.exp(-offset.astype(jnp.float32) / decay_len), jnp.float32(0.0)
     ).astype(jnp.bfloat16)
     near_degree = jnp.sum(band_tiles.astype(jnp.float32), axis=1).reshape(frames)
-    gathered = lax.all_gather(embeddings, "band", axis=0, tiled=True)
+    pile = []
+    for _ in range(lax.axis_size("band")):
+        pile.append(embeddings)
+    oldest = lax.all_to_all(jnp.stack(pile), "band", 0, 0)
+    gathered = jnp.concatenate(oldest, axis=0)
     labels_band = band_gather(arrived.reshape(channels, frames))
     labels_band, gathered = lax.optimization_barrier((labels_band, gathered))
     embed_width = embeddings.shape[1]

time: 343 us -> 468 us (1.36)
  waiting for transfers between devices: 126 us -> 212 us
  blocking collectives: 86.7 us -> 135 us
  between operations: 13.9 us -> 0.52 us
    all_to_all x1, waiting for transfers between devices: 7.39 us -> 168 us  [on_device(): oldest = lax.all_to_all(jnp.stack(pile), 'band', 0, 0)]
    all_gather x1 -> x0, waiting for transfers between devices: 58.1 us -> none  [on_device(): gathered = lax.all_gather(embeddings, 'band', axis=0, tiled=True)]
    all_to_all x0 -> x2, blocking collectives: none -> 46.5 us  [the longest x1 27.4 us: band_gather(): lax.all_to_all(spread, 'band', split_axis=0, concat_axis=0, tiled=True)]
    all_to_all x4 -> x3, waiting for transfers between devices: 53.8 us -> 37.1 us  [band_gather(): lax.all_to_all(spread, 'band', split_axis=0, concat_axis=0, tiled=True)]
    another operation x1 -> x2, local copies, waits for them, and re-layouts: 0.11 us -> 5.22 us  [the longest x1 5.1 us: on_device(): oldest = lax.all_to_all(jnp.stack(pile), 'band', 0, 0)]
    all_to_all x4 -> x3, starting transfers between devices: 17.5 us -> 19.5 us  [band_gather(): lax.all_to_all(spread, 'band', split_axis=0, concat_axis=0, tiled=True)]
  transfers between devices with their start and end apart: 12 -> 10, of which waited for: 8 -> 6; matrix products, arithmetic and copies ran while one was open for 8% -> 4% of each run, Pallas kernels for 0% -> 0%
where the time goes in v1:
time: 468 us; the launch traced here: 467 us
  waiting for transfers between devices  212 us (45%)
  blocking collectives  135 us (29%)
  starting transfers between devices  48 us (10%)
  local copies, waits for them, and re-layouts  44.1 us (9%)
  matrix products  18.2 us (4%)
  other arithmetic  8.91 us (2%)
    all_to_all x1, waiting for transfers between devices, on_device(): oldest = lax.all_to_all(jnp.stack(pile), 'band', 0, 0)  168 us
    all_to_all x6, blocking collectives, total_over_devices(): rows = lax.all_to_all(spread, axis, split_axis=0, concat_axis=0, tiled=True)  88.9 us
    all_to_all x3, waiting for transfers between devices, band_gather(): lax.all_to_all(spread, 'band', split_axis=0, concat_axis=0, tiled=True)  37.1 us
    all_to_all x1, blocking collectives, band_gather(): lax.all_to_all(spread, 'band', split_axis=0, concat_axis=0, tiled=True)  27.4 us
    all_to_all x3, starting transfers between devices, band_gather(): lax.all_to_all(spread, 'band', split_axis=0, concat_axis=0, tiled=True)  19.5 us
    all_to_all x1, blocking collectives, on_device(): lax.all_to_all(ordered, 'band', split_axis=1, concat_axis=1, tiled=True)  19.1 us
    ppermute x3, starting transfers between devices, with_halo(): lax.ppermute(tail, axis, [(i, (i + 1) % count) for i in range(ends)])  14 us
    gather x1, local copies, waits for them, and re-layouts, on_device(): partner_rows = gathered.reshape(-1, 128, embed_width)[partners]  9.99 us
  transfers between devices with their start and end apart: 10, of which 6 were waited for; matrix products, arithmetic and copies ran while one was open for 4% of the time, Pallas kernels for 0%

profile of v1, /device:TPU:1, one launch (start us, length us, event | category | flops | bytes accessed | tf_op | source)
XLA Modules:
  0.0 466.6 jit_solution(6822581995133506168)
XLA Ops:
  0.0 0.7 convert_element_type.66
  0.7 0.8 broadcast_multiply_fusion
  1.6 0.7 compare_select_fusion.1
  2.8 1.3 reduce.14
  4.2 1.3 gather_fusion
  5.9 19.1 %all_to_all.61 = bf16[32,2,256]{2,1,0:T(2,128)(2,1)S(1)} all-to-all(bf16[32,2,256]{2,1,0:T(2,128)(2,1)S(1)} %reshape.835), channel_id=1, replica_groups=mesh['band'=32,'seq'=16] {'band'}, dimensions={0} | all-to-all | bytes 65536 | tf_op jit(solution)/shard_map/all_to_all | solution.py:54
  25.3 27.4 %all_to_all.62 = bf16[32,32,512]{2,1,0:T(8,128)(2,1)S(1)} all-to-all(bf16[32,32,512]{2,1,0:T(8,128)(2,1)S(1)} %broadcast_in_dim.40), channel_id=1, replica_groups=mesh['band'=32,'seq'=16] {'band'}, dimensions={0} | all-to-all | bytes 2097152 | tf_op jit(solution)/shard_map/all_to_all | solution.py:42
  52.7 5.1 %stack.48 = bf16[32,512,256]{2,1,0:T(8,128)(2,1)} broadcast(bf16[512,256]{1,0:T(8,128)(2,1)} %param.11), dimensions={1,2} | broadcast | bytes 8650752 | tf_op jit(solution)/shard_map/stack | solution.py:80
  57.8 8.5 %all-to-all-start.2 = ((bf16[32,512,256]{2,1,0:T(8,128)(2,1)}), bf16[32,512,256]{2,1,0:T(8,128)(2,1)}, u32[]{:S(2)}, u32[]{:S(2)}) async-start(bf16[32,512,256]{2,1,0:T(8,128)(2,1)} %stack.48), calls=%async_computation.2 | async-start | bytes 16777216 | tf_op jit(solution)/shard_map/all_to_all | solution.py:80
  67.3 4.5 gather_fusion.1
  71.9 2.3 gather_fusion.2
  74.2 6.8 %gather_fusion.3 = pred[1024]{0:T(1024)(128)(4,1)S(1)} fusion(pred[640]{0:T(1024)(128)(4,1)S(1)} %compare_and_fusion.1, s32[1024]{0:T(1024)S(1)} %broadcast_clamp_fusion), kind=kCustom, calls=%fused_computation.3 | custom fusion | bytes 6144 | tf_op jit(solution)/shard_map/gather | solution.py:71
  81.9 168.1 %all-to-all-done.2 = bf16[32,512,256]{2,1,0:T(8,128)(2,1)} async-done(((bf16[32,512,256]{2,1,0:T(8,128)(2,1)}), bf16[32,512,256]{2,1,0:T(8,128)(2,1)}, u32[]{:S(2)}, u32[]{:S(2)}) %all-to-all-start.2) | async-done | bytes 8388640 | tf_op jit(solution)/shard_map/all_to_all | solution.py:80
  250.0 10.0 %gather_fusion.4 = bf16[128,128,256]{2,1,0:T(8,128)(2,1)} fusion(bf16[128,128,256]{2,1,0:T(8,128)(2,1)} %bitcast.10, s32[1024]{0:T(1024)S(1)} %pad_clamp_fusion), kind=kCustom, calls=%fused_computation.4 | custom fusion | bytes 16777728 | tf_op jit(solution)/shard_map/gather | solution.py:85
  259.9 7.7 %convert_reduce_fusion = (f32[4,128]{1,0:T(4,128)S(1)}, bf16[4,32,128,128]{3,2,1,0:T(8,128)(2,1)}) fusion(f32[4,32]{1,0:T(4,128)S(1)} %convert_multiply_fusion.6, bf16[4,32,128,256]{3,2,1,0:T(8,128)(2,1)} %bitcast.182, bf16[4,128,256,1]{2,1,3,0:T(8,128)(2,1)S(1)} %bitcast.197), kind=kOutput, calls=%fused_computation.8 | convolution fusion | flops 1086324224 | bytes 12847616 | tf_op jit(solution)/shard_map/tkje,tie->tkji/dot_general | solution.py:87
  267.7 6.1 %collective-permute-start = (bf16[32,64]{1,0:T(8,128)(2,1)S(1)}, bf16[32,64]{1,0:T(8,128)(2,1)S(1)}, u32[]{:S(2)}, u32[]{:S(2)}) collective-permute-start(bf16[32,64]{1,0:T(8,128)(2,1)S(1)} %get-tuple-element.41), channel_id=1, source_target_pairs={{0,1},{1,2},{2,3},{3,4},{4,5},{5,6},{6,7},{7,8},{8,9},{9,10},{10,1... | collective-permute-start | bytes 12296 | tf_op jit(solution)/shard_map/ppermute | solution.py:21
  273.9 1.9 collective-permute-start.1
  276.5 11.6 %all-to-all-start.3 = ((f32[32,1,512]{2,1,0:T(1,128)}), f32[32,1,512]{2,1,0:T(1,128)S(1)}, u32[]{:S(2)}, u32[]{:S(2)}) async-start(f32[32,1,512]{2,1,0:T(1,128)} %mul.397), calls=%async_computation.3 | async-start | bytes 131072 | tf_op jit(solution)/shard_map/all_to_all | solution.py:42
  288.9 7.9 %all-to-all-done.3 = f32[32,1,512]{2,1,0:T(1,128)S(1)} async-done(((f32[32,1,512]{2,1,0:T(1,128)}), f32[32,1,512]{2,1,0:T(1,128)S(1)}, u32[]{:S(2)}, u32[]{:S(2)}) %all-to-all-start.3) | async-done | bytes 65568 | tf_op jit(solution)/shard_map/all_to_all | solution.py:42
  298.3 0.7 copy.75
  299.0 0.8 gather_fusion.5
  299.7 2.9 fusion.3
  303.1 19.5 %all_to_all.63 = f32[16,1,128]{2,1,0:T(1,128)S(1)} all-to-all(f32[16,1,128]{2,1,0:T(1,128)S(1)} %reshape.837), channel_id=1, replica_groups=mesh['band'=32,'seq'=16] {'seq'}, dimensions={0} | all-to-all | bytes 16384 | tf_op jit(solution)/shard_map/all_to_all | solution.py:34
  324.0 11.6 %all_to_all.64 = f32[32,1,128]{2,1,0:T(1,128)S(1)} all-to-all(f32[32,1,128]{2,1,0:T(1,128)S(1)} %reshape.839), channel_id=1, replica_groups=mesh['band'=32,'seq'=16] {'band'}, dimensions={0} | all-to-all | bytes 32768 | tf_op jit(solution)/shard_map/all_to_all | solution.py:34
  335.6 0.7 reduce.16
  336.6 1.1 broadcast_in_dim.44
  337.7 3.9 all-to-all-start.6
  341.7 4.0 collective-permute-start.2
  345.7 1.9 collective-permute-start.3
  347.7 3.3 collective-permute-done.3
  351.7 14.5 %all-to-all-done.6 = bf16[32,32,512]{2,1,0:T(8,128)(2,1)S(1)} async-done(((bf16[32,32,512]{2,1,0:T(8,128)(2,1)}), bf16[32,32,512]{2,1,0:T(8,128)(2,1)S(1)}, u32[]{:S(2)}, u32[]{:S(2)}) %all-to-all-start.6) | async-done | bytes 1048608 | tf_op jit(solution)/shard_map/all_to_all | solution.py:42
  367.4 0.7 copy.81
  368.1 0.8 gather_fusion.6
  368.9 2.9 fusion.2
  372.2 15.1 %all_to_all.65 = f32[16,3,32]{2,1,0:T(4,128)S(1)} all-to-all(f32[16,3,32]{2,1,0:T(4,128)S(1)} %broadcast_in_dim.45), channel_id=1, replica_groups=mesh['band'=32,'seq'=16] {'seq'}, dimensions={0} | all-to-all | bytes 12288 | tf_op jit(solution)/shard_map/all_to_all | solution.py:34
  387.3 14.1 %all_to_all.66 = f32[32,3,32]{2,1,0:T(4,128)S(1)} all-to-all(f32[32,3,32]{2,1,0:T(4,128)S(1)} %broadcast_in_dim.46), channel_id=1, replica_groups=mesh['band'=32,'seq'=16] {'band'}, dimensions={0} | all-to-all | bytes 24576 | tf_op jit(solution)/shard_map/all_to_all | solution.py:34
  401.6 1.1 broadcast_in_dim.47
  402.7 3.9 all-to-all-start.9
  406.7 3.9 collective-permute-start.4
  410.6 2.1 collective-permute-start.5
  412.8 3.1 collective-permute-done.5
  416.6 14.7 %all-to-all-done.9 = bf16[32,32,512]{2,1,0:T(8,128)(2,1)S(1)} async-done(((bf16[32,32,512]{2,1,0:T(8,128)(2,1)}), bf16[32,32,512]{2,1,0:T(8,128)(2,1)S(1)}, u32[]{:S(2)}, u32[]{:S(2)}) %all-to-all-start.9) | async-done | bytes 1048608 | tf_op jit(solution)/shard_map/all_to_all | solution.py:42
  432.5 0.7 copy.87
  433.2 0.8 gather_fusion.7
  434.0 2.9 fusion.1
  437.3 14.7 %all_to_all.67 = f32[16,1,32]{2,1,0:T(1,128)S(1)} all-to-all(f32[16,1,32]{2,1,0:T(1,128)S(1)} %broadcast_in_dim.48), channel_id=1, replica_groups=mesh['band'=32,'seq'=16] {'seq'}, dimensions={0} | all-to-all | bytes 4096 | tf_op jit(solution)/shard_map/all_to_all | solution.py:34
  452.0 13.9 %all_to_all.68 = f32[32,1,32]{2,1,0:T(1,128)S(1)} all-to-all(f32[32,1,32]{2,1,0:T(1,128)S(1)} %broadcast_in_dim.49), channel_id=1, replica_groups=mesh['band'=32,'seq'=16] {'band'}, dimensions={0} | all-to-all | bytes 8192 | tf_op jit(solution)/shard_map/all_to_all | solution.py:34
  465.9 0.7 fusion.19
  (99 shorter events, 13.4 us)
Async XLA Ops:
  57.8 8.5 %copy-start.3 = (s32[256]{0:T(256)S(1)}, s32[256]{0:T(256)}, u32[]{:S(2)}) copy-start(s32[256]{0:T(256)} %param.10) | copy-start | bytes 3076
  57.8 23.3 %copy-start.1 = (s32[4,32]{1,0:T(4,128)S(1)}, s32[4,32]{1,0:T(4,128)}, u32[]{:S(2)}) copy-start(s32[4,32]{1,0:T(4,128)} %param.12) | copy-start | bytes 1540
  57.8 24.1 %copy-start.2 = (s32[4,32]{1,0:T(4,128)S(1)}, s32[4,32]{1,0:T(4,128)}, u32[]{:S(2)}) copy-start(s32[4,32]{1,0:T(4,128)} %param.13) | copy-start | bytes 1540
  57.8 192.2 %all-to-all-start.2 = ((bf16[32,512,256]{2,1,0:T(8,128)(2,1)}), bf16[32,512,256]{2,1,0:T(8,128)(2,1)}, u32[]{:S(2)}, u32[]{:S(2)}) async-start(bf16[32,512,256]{2,1,0:T(8,128)(2,1)} %stack.48), calls=%async_computation.2 | async-start | bytes 16777216 | tf_op jit(solution)/shard_map/all_to_all | solution.py:80
  250.0 10.0 %copy-start = (bf16[512,256]{1,0:T(8,128)(2,1)S(1)}, bf16[512,256]{1,0:T(8,128)(2,1)}, u32[]{:S(2)}) copy-start(bf16[512,256]{1,0:T(8,128)(2,1)} %param.11) | copy-start | bytes 786436
  267.7 20.4 %collective-permute-start = (bf16[32,64]{1,0:T(8,128)(2,1)S(1)}, bf16[32,64]{1,0:T(8,128)(2,1)S(1)}, u32[]{:S(2)}, u32[]{:S(2)}) collective-permute-start(bf16[32,64]{1,0:T(8,128)(2,1)S(1)} %get-tuple-element.41), channel_id=1, source_target_pairs={{0,1},{1,2},{2,3},{3,4},{4,5},{5,6},{6,7},{7,8},{8,9},{9,10},{10,1... | collective-permute-start | bytes 12296 | tf_op jit(solution)/shard_map/ppermute | solution.py:21
  273.9 14.3 %collective-permute-start.1 = (bf16[32,64]{1,0:T(8,128)(2,1)S(1)}, bf16[32,64]{1,0:T(8,128)(2,1)S(1)}, u32[]{:S(2)}, u32[]{:S(2)}) collective-permute-start(bf16[32,64]{1,0:T(8,128)(2,1)S(1)} %get-tuple-element.42), channel_id=1, source_target_pairs={{1,0},{2,1},{3,2},{4,3},{5,4},{6,5},{7,6},{8,7},{9,8},{10,9},{11,1... | collective-permute-start | bytes 12296 | tf_op jit(solution)/shard_map/ppermute | solution.py:23
  276.5 20.3 %all-to-all-start.3 = ((f32[32,1,512]{2,1,0:T(1,128)}), f32[32,1,512]{2,1,0:T(1,128)S(1)}, u32[]{:S(2)}, u32[]{:S(2)}) async-start(f32[32,1,512]{2,1,0:T(1,128)} %mul.397), calls=%async_computation.3 | async-start | bytes 131072 | tf_op jit(solution)/shard_map/all_to_all | solution.py:42
  337.7 28.5 %all-to-all-start.6 = ((bf16[32,32,512]{2,1,0:T(8,128)(2,1)}), bf16[32,32,512]{2,1,0:T(8,128)(2,1)S(1)}, u32[]{:S(2)}, u32[]{:S(2)}) async-start(bf16[32,32,512]{2,1,0:T(8,128)(2,1)} %broadcast_in_dim.44), calls=%async_computation.6 | async-start | bytes 2097152 | tf_op jit(solution)/shard_map/all_to_all | solution.py:42
  341.7 6.0 %collective-permute-start.2 = (bf16[32,64]{1,0:T(8,128)(2,1)S(1)}, bf16[32,64]{1,0:T(8,128)(2,1)S(1)}, u32[]{:S(2)}, u32[]{:S(2)}) collective-permute-start(bf16[32,64]{1,0:T(8,128)(2,1)S(1)} %get-tuple-element.35), channel_id=1, source_target_pairs={{0,1},{1,2},{2,3},{3,4},{4,5},{5,6},{6,7},{7,8},{8,9},{9,10},{10,1... | collective-permute-start | bytes 12296 | tf_op jit(solution)/shard_map/ppermute | solution.py:21
  345.7 5.3 %collective-permute-start.3 = (bf16[32,64]{1,0:T(8,128)(2,1)S(1)}, bf16[32,64]{1,0:T(8,128)(2,1)S(1)}, u32[]{:S(2)}, u32[]{:S(2)}) collective-permute-start(bf16[32,64]{1,0:T(8,128)(2,1)S(1)} %get-tuple-element.36), channel_id=1, source_target_pairs={{1,0},{2,1},{3,2},{4,3},{5,4},{6,5},{7,6},{8,7},{9,8},{10,9},{11,1... | collective-permute-start | bytes 12296 | tf_op jit(solution)/shard_map/ppermute | solution.py:23
  402.7 28.5 %all-to-all-start.9 = ((bf16[32,32,512]{2,1,0:T(8,128)(2,1)}), bf16[32,32,512]{2,1,0:T(8,128)(2,1)S(1)}, u32[]{:S(2)}, u32[]{:S(2)}) async-start(bf16[32,32,512]{2,1,0:T(8,128)(2,1)} %broadcast_in_dim.47), calls=%async_computation.9 | async-start | bytes 2097152 | tf_op jit(solution)/shard_map/all_to_all | solution.py:42
  406.7 6.0 %collective-permute-start.4 = (bf16[32,64]{1,0:T(8,128)(2,1)S(1)}, bf16[32,64]{1,0:T(8,128)(2,1)S(1)}, u32[]{:S(2)}, u32[]{:S(2)}) collective-permute-start(bf16[32,64]{1,0:T(8,128)(2,1)S(1)} %get-tuple-element.29), channel_id=1, source_target_pairs={{0,1},{1,2},{2,3},{3,4},{4,5},{5,6},{6,7},{7,8},{8,9},{9,10},{10,1... | collective-permute-start | bytes 12296 | tf_op jit(solution)/shard_map/ppermute | solution.py:21
  410.6 5.3 %collective-permute-start.5 = (bf16[32,64]{1,0:T(8,128)(2,1)S(1)}, bf16[32,64]{1,0:T(8,128)(2,1)S(1)}, u32[]{:S(2)}, u32[]{:S(2)}) collective-permute-start(bf16[32,64]{1,0:T(8,128)(2,1)S(1)} %get-tuple-element.30), channel_id=1, source_target_pairs={{1,0},{2,1},{3,2},{4,3},{5,4},{6,5},{7,6},{8,7},{9,8},{10,9},{11,1... | collective-permute-start | bytes 12296 | tf_op jit(solution)/shard_map/ppermute | solution.py:23
